TPU v7x, 32 devices: a whole 2x2x4 slice. The times are simulated.
32 devices in a mesh: row: 8 (over z, y), col: 4 (over x, core).
Axes of the slice: x: 2, y: 2, z: 4, core: 2. Of those that a mesh axis runs over, the one named last changes fastest.
Arguments:
- density: float32 [4, 256, 2048], P('col', 'row'), may hold values from 0.5 to 2
- momentum: float32 [3, 4, 256, 2048], P(None, 'col', 'row'), may hold values from -6 to 6
- energy: float32 [4, 256, 2048], P('col', 'row'), may hold values from 2 to 5
Outputs:
- tendency: float32 [5, 4, 256, 2048], P(None, 'col', 'row')
All inputs are finite; a program needn't handle non-finite values.
Results may differ from a plain program's by a relative error of at most 0.000053.
Values sent between devices are 32-bit elements; how exact they have to be, the bound alone decides.
No kernel may reach another device: no remote copies, remote signals or barrier semaphores. Data moves between devices by JAX's collectives and lax.ppermute only.
A program may use at most 64 MiB of HBM per device.

v0:
```python
import jax
import jax.numpy as jnp
import numpy as np
from jax import lax
from jax.sharding import PartitionSpec as P


def operator_column(count):
    steps = np.arange(count)
    wave = 2.0 * np.pi * steps / count
    upper = (
        17.0 / 12.0 * np.sin(wave)
        + 101.0 / 300.0 * np.sin(2.0 * wave)
        + 1.0 / 300.0 * np.sin(3.0 * wave)
    )
    lower = 1.0 + np.cos(wave) + 0.1 * np.cos(2.0 * wave)
    ratio = upper / lower
    phase = 2.0 * np.pi * (steps[:, None] * steps[None, :] % count) / count
    return -np.sum(ratio[:, None] * np.sin(phase), axis=0) / count


def operator_table(count):
    column = operator_column(count)
    steps = np.arange(count)
    offsets = (steps[None, :] - steps[:, None]) % count
    return column[offsets].astype(np.float32)


def block_weights(count):
    table = operator_table(count)
    width = 128
    w_self = table[:width, :width]
    w_prev = table[:width, width : 2 * width]
    w_next = table[width : 2 * width, :width]
    return jnp.asarray(np.concatenate([w_prev, w_self, w_next], axis=1))


def compact_last(field):
    count = field.shape[-1]
    width = 128
    blocks = field.reshape(field.shape[:-1] + (count // width, width))
    parts = jnp.einsum(
        "...bj,jk->...bk", blocks, block_weights(count), precision=lax.Precision.HIGHEST
    )
    result = (
        jnp.roll(parts[..., :width], 1, axis=-2)
        + parts[..., width : 2 * width]
        + jnp.roll(parts[..., 2 * width :], -1, axis=-2)
    )
    return result.reshape(field.shape)


def compact_second(field):
    count = field.shape[-2]
    if count <= 256:
        weights = jnp.asarray(operator_table(count))
        return jnp.einsum("...jc,ji->...ic", field, weights, precision=lax.Precision.HIGHEST)
    width = 128
    blocks = field.reshape(field.shape[:-2] + (count // width, width, field.shape[-1]))
    parts = jnp.einsum(
        "...bjc,jk->...bkc", blocks, block_weights(count), precision=lax.Precision.HIGHEST
    )
    result = (
        jnp.roll(parts[..., :width, :], 1, axis=-3)
        + parts[..., width : 2 * width, :]
        + jnp.roll(parts[..., 2 * width :, :], -1, axis=-3)
    )
    return result.reshape(field.shape)


def fluxes(density, momentum, energy):
    speed = momentum / density[None]
    pressure = 0.4 * (energy - 0.5 * jnp.sum(momentum * momentum, axis=0) / density)
    enthalpy = energy + pressure
    vel_x, vel_y = (speed[0], speed[1])
    flux_x = jnp.stack(
        [
            momentum[0],
            momentum[0] * vel_x + pressure,
            momentum[1] * vel_x,
            momentum[2] * vel_x,
            enthalpy * vel_x,
        ]
    )
    flux_y = jnp.stack(
        [
            momentum[1],
            momentum[0] * vel_y,
            momentum[1] * vel_y + pressure,
            momentum[2] * vel_y,
            enthalpy * vel_y,
        ],
        axis=2,
    )
    return (flux_x, flux_y)


def local(density, momentum, energy):
    flux_x, flux_y = fluxes(density, momentum, energy)
    planes, owned, length = (flux_y.shape[0], flux_y.shape[1], flux_y.shape[3])
    packed = flux_y.reshape(planes, owned, 5 * length)
    derivative_x = compact_last(flux_x)
    y_lines = lax.all_to_all(packed, "row", split_axis=2, concat_axis=1, tiled=True)
    derivative_lines = compact_second(y_lines)
    derived = lax.all_to_all(derivative_lines, "row", split_axis=1, concat_axis=2, tiled=True)
    derivative_y = jnp.transpose(derived.reshape(planes, owned, 5, length), (2, 0, 1, 3))
    return -(derivative_x + derivative_y)


def solution(mesh):
    in_specs = (P("col", "row", None), P(None, "col", "row", None), P("col", "row", None))
    out_specs = P(None, "col", "row", None)
    return jax.shard_map(local, mesh=mesh, in_specs=in_specs, out_specs=out_specs, check_vma=False)
```

profile of v0, /device:TPU:0, one launch (start us, length us, event | category | flops | bytes accessed | tf_op | source)
XLA Modules:
  0.0 174.0 jit_solution(4821467168655819884)
XLA Ops:
  0.0 0.0 copy-start
  0.0 1.0 bitcast_dynamic-update-slice_fusion.9
  1.0 0.0 copy-start.1
  1.1 0.0 copy-start.2
  1.1 1.4 multiply_reduce_fusion
  2.5 0.0 copy-done
  2.5 0.0 copy-done.1
  2.5 0.0 copy-done.2
  2.5 0.1 bitcast_dynamic-update-slice_fusion.7
  2.7 3.8 %copy.31 = f32[1,32,5,2048]{1,3,2,0:T(8,128)} copy(f32[1,32,5,2048]{3,1,2,0:T(8,128)S(1)} %bitcast_dynamic-update-slice_fusion.5) | data formatting | bytes 2621440 | tf_op jit(solution)/shard_map/reshape | solution.py:101
  6.5 0.5 broadcast.11
  7.0 47.4 %reduce.1 = f32[10240,32]{1,0:T(8,128)} reduce(f32[10240,1,32]{2,1,0:T(1,128)} %bitcast.106, f32[]{:T(128)} %broadcast.11), dimensions={1}, to_apply=%bitcast.93.reduce_sub_computation | reduce | bytes 2621444
  54.4 5.3 %reshape.146 = f32[8,1,40960]{2,1,0:T(1,128)} reshape(f32[10240,32]{1,0:T(8,128)} %reduce.1) | data formatting | bytes 2621440
  59.8 38.7 %all_to_all.30 = f32[8,1,40960]{2,1,0:T(1,128)S(1)} all-to-all(f32[8,1,40960]{2,1,0:T(1,128)} %reshape.146), channel_id=1, replica_groups=mesh['row'=8,'col'=4] {'row'}, dimensions={0} | all-to-all | bytes 2621440 | tf_op jit(solution)/shard_map/all_to_all | solution.py:103
  98.4 5.2 %reduce.2 = f32[8,40960]{1,0:T(8,128)} reduce(f32[8,1,40960]{2,1,0:T(1,128)S(1)} %all_to_all.30, f32[]{:T(128)} %broadcast.11), dimensions={1}, to_apply=%all_to_all.22.reduce_sub_computation | reduce | bytes 2621444 | tf_op jit(solution)/shard_map/all_to_all | solution.py:103
  103.7 12.0 %reshape.147 = f32[10240,1,32]{2,1,0:T(1,128)} reshape(f32[8,40960]{1,0:T(8,128)} %reduce.2) | data formatting | bytes 2621440
  115.6 10.6 %copy.26 = f32[1,32,10240]{2,1,0:T(8,128)} copy(f32[1,32,10240]{1,0,2:T(1,128)} %bitcast.107) | data formatting | bytes 2621440 | tf_op jit(solution)/shard_map/all_to_all | solution.py:103
  126.2 1.5 reshape.141
  127.8 2.2 %convolution_bitcast_fusion = f32[1,256,1280]{2,1,0:T(8,128)S(1)} fusion(f32[256,256]{1,0:T(8,128)} %constant.17, f32[256,1280]{1,0:T(8,128)S(1)} %reshape.141), kind=kOutput, calls=%fused_computation | convolution fusion | flops 1006632960 | bytes 2883584 | tf_op jit(solution)/shard_map/...jc,ji->...ic/dot_general | solution.py:57
  130.0 2.4 %copy.27 = f32[1,256,1280]{2,0,1:T(1,128)} copy(f32[1,256,1280]{2,1,0:T(8,128)S(1)} %convolution_bitcast_fusion) | data formatting | bytes 2621440 | tf_op jit(solution)/shard_map/...jc,ji->...ic/transpose | solution.py:57
  132.4 4.3 %all-to-all-start.1 = ((f32[1,256,1280]{2,0,1:T(1,128)}), f32[1,256,1280]{2,0,1:T(1,128)}, u32[]{:S(2)}, u32[]{:S(2)}) async-start(f32[1,256,1280]{2,0,1:T(1,128)} %copy.27), calls=%async_computation.1 | async-start | bytes 2621440 | tf_op jit(solution)/shard_map/all_to_all | solution.py:105
  136.6 0.1 multiply_bitcast_fusion
  136.9 0.1 fusion.7
  137.1 0.0 copy-start.3
  137.2 0.8 copy-done.3
  138.0 3.5 %convolution_bitcast_fusion.1 = f32[5,1,32,16,384]{4,3,2,0,1:T(8,128)S(1)} fusion(f32[5,32,16,128]{3,2,1,0:T(8,128)S(1)} %bitcast_dynamic-update-slice_fusion, f32[128,384,1,1]{1,0,3,2:T(8,128)S(1)} %copy-done.3), kind=kOutput, calls=%fused_computation.1 | convolution fusion | flops 1509949440 | bytes 5439488 | tf_op jit(solution)/shard_map/...bj,jk->...bk/dot_general | solution.py:42
  141.5 0.1 fusion.10
  141.6 0.2 fusion.9
  141.9 0.4 fusion
  142.2 0.2 reshape.137
  142.4 24.9 %all-to-all-done.1 = f32[1,256,1280]{2,0,1:T(1,128)} async-done(((f32[1,256,1280]{2,0,1:T(1,128)}), f32[1,256,1280]{2,0,1:T(1,128)}, u32[]{:S(2)}, u32[]{:S(2)}) %all-to-all-start.1) | async-done | bytes 1310752 | tf_op jit(solution)/shard_map/all_to_all | solution.py:105
  167.3 3.1 %copy.40 = f32[1,8,32,1280]{3,1,2,0:T(8,128)} copy(f32[1,8,32,1280]{3,0,2,1:T(1,128)} %bitcast.16) | data formatting | bytes 2621440 | tf_op jit(solution)/shard_map/all_to_all | solution.py:105
  170.5 1.5 reshape.140
  172.0 2.0 %fusion.1 = f32[5,1,32,2048]{3,2,1,0:T(8,128)} fusion(f32[5,1,32,2048]{3,2,1,0:T(8,128)S(1)} %reshape.137, f32[1,32,5,2048]{3,2,1,0:T(8,128)S(1)} %reshape.140), kind=kLoop, calls=%fused_computation.5 | loop fusion | flops 655360 | bytes 3932160 | tf_op jit(solution)/shard_map/neg | solution.py:107
  (13 shorter events, 0.4 us)
Async XLA Ops:
  0.0 2.5 %copy-start = (f32[3,1,32,2048]{3,2,1,0:T(8,128)S(1)}, f32[3,1,32,2048]{3,2,1,0:T(8,128)}, u32[]{:S(2)}) copy-start(f32[3,1,32,2048]{3,2,1,0:T(8,128)} %param.6) | copy-start | bytes 2359300
  1.0 1.5 copy-start.1
  1.1 1.5 copy-start.2
  132.4 35.0 %all-to-all-start.1 = ((f32[1,256,1280]{2,0,1:T(1,128)}), f32[1,256,1280]{2,0,1:T(1,128)}, u32[]{:S(2)}, u32[]{:S(2)}) async-start(f32[1,256,1280]{2,0,1:T(1,128)} %copy.27), calls=%async_computation.1 | async-start | bytes 2621440 | tf_op jit(solution)/shard_map/all_to_all | solution.py:105
  137.1 0.9 copy-start.3
where the time goes:
time: 175 us; the launch traced here: 174 us
  other arithmetic  56.7 us (32%)
  local copies, waits for them, and re-layouts  43.5 us (25%)
  blocking collectives  38.7 us (22%)
  waiting for transfers between devices  24.9 us (14%)
  matrix products  5.71 us (3%)
  starting transfers between devices  4.26 us (2%)
    unnamed x6, other arithmetic  47.7 us
    all_to_all x1, blocking collectives, local(): lax.all_to_all(packed, 'row', split_axis=2, concat_axis=1, tiled=True)  38.7 us
    all_to_all x1, waiting for transfers between devices, local(): lax.all_to_all(derivative_lines, 'row', split_axis=1, concat_axis=2, tile...  24.9 us
    unnamed x21, local copies, waits for them, and re-layouts  20 us
    all_to_all x1, local copies, waits for them, and re-layouts, local(): lax.all_to_all(packed, 'row', split_axis=2, concat_axis=1, tiled=True)  10.6 us
    all_to_all x1, other arithmetic, local(): lax.all_to_all(packed, 'row', split_axis=2, concat_axis=1, tiled=True)  5.24 us
    all_to_all x1, starting transfers between devices, local(): lax.all_to_all(derivative_lines, 'row', split_axis=1, concat_axis=2, tile...  4.26 us
    reshape x1, local copies, waits for them, and re-layouts, local(): packed = flux_y.reshape(planes, owned, 5 * length)  3.76 us
  transfers between devices with their start and end apart: 1, of which 1 were waited for; matrix products, arithmetic and copies ran while one was open for 3% of the time, Pallas kernels for 0%

commit v1 on v0

--- a/solution.py
+++ b/solution.py
@@ -3,6 +3,17 @@
 import numpy as np
 from jax import lax
 from jax.sharding import PartitionSpec as P
+
+
+def cut_along(x, dim, size):
+    before, after = (x.shape[:dim], x.shape[dim + 1 :])
+    return jnp.moveaxis(x.reshape(*before, size, -1, *after), dim, 0)
+
+
+def joined_along(parts, dim):
+    parts = jnp.moveaxis(parts, 0, dim)
+    shape = parts.shape
+    return parts.reshape(*shape[:dim], shape[dim] * shape[dim + 1], *shape[dim + 2 :])
 
 
 def operator_column(count):
@@ -102,7 +113,14 @@
     derivative_x = compact_last(flux_x)
     y_lines = lax.all_to_all(packed, "row", split_axis=2, concat_axis=1, tiled=True)
     derivative_lines = compact_second(y_lines)
-    derived = lax.all_to_all(derivative_lines, "row", split_axis=1, concat_axis=2, tiled=True)
+    length_2, index = (lax.axis_size("row"), lax.axis_index("row"))
+    pieces = cut_along(derivative_lines, 1, length_2)
+    gathered = [pieces[index]]
+    for step in range(1, length_2):
+        sent = pieces[index ^ step]
+        gathered.append(lax.ppermute(sent, "row", [(i, i ^ step) for i in range(length_2)]))
+    pieces = jnp.stack(gathered)[index ^ jnp.arange(length_2)]
+    derived = joined_along(pieces, 2)
     derivative_y = jnp.transpose(derived.reshape(planes, owned, 5, length), (2, 0, 1, 3))
     return -(derivative_x + derivative_y)
 

time: 175 us -> 166 us (0.949)
  blocking collectives: 38.7 us -> 0 us
  waiting for transfers between devices: 24.9 us -> 41.1 us
  starting transfers between devices: 4.26 us -> 17.3 us
    all_to_all x1 -> x0, blocking collectives: 38.7 us -> none  [local(): lax.all_to_all(packed, 'row', split_axis=2, concat_axis=1, tiled=True)]
    ppermute x0 -> x7, waiting for transfers between devices: none -> 16.4 us  [local(): lax.ppermute(sent, 'row', [(i, i ^ step) for i in range(length_2)])]
    ppermute x0 -> x7, starting transfers between devices: none -> 10 us  [local(): lax.ppermute(sent, 'row', [(i, i ^ step) for i in range(length_2)])]
    unnamed x21 -> x31, local copies, waits for them, and re-layouts: 20 us -> 24.6 us
    all_to_all x1 -> x0, local copies, waits for them, and re-layouts: 3.13 us -> none  [local(): lax.all_to_all(derivative_lines, 'row', split_axis=1, concat_axis=2, tile...]
    all_to_all x1, starting transfers between devices: 4.26 us -> 7.28 us  [local(): lax.all_to_all(packed, 'row', split_axis=2, concat_axis=1, tiled=True)]
    another operation x0 -> x2, local copies, waits for them, and re-layouts: none -> 2.23 us  [the longest x1 1.54 us: local(): derived.reshape(planes, owned, 5, length)]
    gather x0 -> x1, local copies, waits for them, and re-layouts: none -> 1.95 us  [local(): pieces = jnp.stack(gathered)[index ^ jnp.arange(length_2)]]
  transfers between devices with their start and end apart: 1 -> 8, of which waited for: 1 -> 4; matrix products, arithmetic and copies ran while one was open for 3% -> 7% of each run, Pallas kernels for 0% -> 0%
where the time goes in v1:
time: 166 us; the launch traced here: 165 us
  other arithmetic  56.1 us (34%)
  local copies, waits for them, and re-layouts  45.1 us (27%)
  waiting for transfers between devices  41.1 us (25%)
  starting transfers between devices  17.3 us (10%)
  matrix products  4.74 us (3%)
    unnamed x6, other arithmetic  47.6 us
    all_to_all x1, waiting for transfers between devices, local(): lax.all_to_all(packed, 'row', split_axis=2, concat_axis=1, tiled=True)  24.7 us
    unnamed x31, local copies, waits for them, and re-layouts  24.6 us
    ppermute x7, waiting for transfers between devices, local(): lax.ppermute(sent, 'row', [(i, i ^ step) for i in range(length_2)])  16.4 us
    ppermute x7, starting transfers between devices, local(): lax.ppermute(sent, 'row', [(i, i ^ step) for i in range(length_2)])  10 us
    all_to_all x1, local copies, waits for them, and re-layouts, local(): lax.all_to_all(packed, 'row', split_axis=2, concat_axis=1, tiled=True)  9.2 us
    all_to_all x1, starting transfers between devices, local(): lax.all_to_all(packed, 'row', split_axis=2, concat_axis=1, tiled=True)  7.28 us
    reshape x1, local copies, waits for them, and re-layouts, local(): packed = flux_y.reshape(planes, owned, 5 * length)  3.7 us
  transfers between devices with their start and end apart: 8, of which 4 were waited for; matrix products, arithmetic and copies ran while one was open for 7% of the time, Pallas kernels for 0%

profile of v1, /device:TPU:0, one launch (start us, length us, event | category | flops | bytes accessed | tf_op | source)
XLA Modules:
  0.0 164.7 jit_solution(4018534087454543467)
XLA Ops:
  0.0 1.0 bitcast_dynamic-update-slice_fusion.9
  1.1 1.4 multiply_reduce_fusion
  2.5 0.1 bitcast_dynamic-update-slice_fusion.7
  2.7 3.7 %copy.31 = f32[1,32,5,2048]{1,3,2,0:T(8,128)} copy(f32[1,32,5,2048]{3,1,2,0:T(8,128)S(1)} %bitcast_dynamic-update-slice_fusion.5) | data formatting | bytes 2621440 | tf_op jit(solution)/shard_map/reshape | solution.py:112
  6.4 0.5 broadcast.46
  6.9 47.4 %reduce.1 = f32[10240,32]{1,0:T(8,128)} reduce(f32[10240,1,32]{2,1,0:T(1,128)} %bitcast.135, f32[]{:T(128)} %broadcast.46), dimensions={1}, to_apply=%bitcast.123.reduce_sub_computation | reduce | bytes 2621444
  54.3 5.3 %reshape.167 = f32[8,1,40960]{2,1,0:T(1,128)} reshape(f32[10240,32]{1,0:T(8,128)} %reduce.1) | data formatting | bytes 2621440
  59.6 7.3 %all-to-all-start = ((f32[8,1,40960]{2,1,0:T(1,128)}), f32[8,1,40960]{2,1,0:T(1,128)S(1)}, u32[]{:S(2)}, u32[]{:S(2)}) async-start(f32[8,1,40960]{2,1,0:T(1,128)} %reshape.167), calls=%async_computation | async-start | bytes 2621440 | tf_op jit(solution)/shard_map/all_to_all | solution.py:114
  66.9 0.1 fusion.7
  67.0 0.1 multiply_bitcast_fusion
  67.3 0.0 copy-start.5
  67.5 0.8 copy-done.5
  68.3 3.5 %convolution_bitcast_fusion = f32[5,1,32,16,384]{4,3,2,0,1:T(8,128)S(1)} fusion(f32[5,32,16,128]{3,2,1,0:T(8,128)S(1)} %bitcast_dynamic-update-slice_fusion, f32[128,384,1,1]{1,0,3,2:T(8,128)S(1)} %copy-done.5), kind=kOutput, calls=%fused_computation.1 | convolution fusion | flops 1509949440 | bytes 5439488 | tf_op jit(solution)/shard_map/...bj,jk->...bk/dot_general | solution.py:53
  71.8 0.1 fusion.11
  71.9 0.2 fusion.10
  72.1 1.4 fusion
  73.6 24.7 %all-to-all-done = f32[8,1,40960]{2,1,0:T(1,128)S(1)} async-done(((f32[8,1,40960]{2,1,0:T(1,128)}), f32[8,1,40960]{2,1,0:T(1,128)S(1)}, u32[]{:S(2)}, u32[]{:S(2)}) %all-to-all-start) | async-done | bytes 1310752 | tf_op jit(solution)/shard_map/all_to_all | solution.py:114
  98.3 3.7 %reduce.2 = f32[8,40960]{1,0:T(8,128)S(1)} reduce(f32[8,1,40960]{2,1,0:T(1,128)S(1)} %all-to-all-done, f32[]{:T(128)} %broadcast.46), dimensions={1}, to_apply=%all_to_all.11.reduce_sub_computation | reduce | bytes 2621444 | tf_op jit(solution)/shard_map/all_to_all | solution.py:114
  102.0 10.9 %reshape.168 = f32[10240,1,32]{2,1,0:T(1,128)} reshape(f32[8,40960]{1,0:T(8,128)S(1)} %reduce.2) | data formatting | bytes 2621440
  112.8 9.2 %copy.27 = f32[1,32,10240]{2,1,0:T(8,128)S(1)} copy(f32[1,32,10240]{1,0,2:T(1,128)} %bitcast.136) | data formatting | bytes 2621440 | tf_op jit(solution)/shard_map/all_to_all | solution.py:114
  122.0 0.0 copy-start.4
  122.0 0.2 reshape.152
  122.2 0.7 copy-done.4
  123.0 1.2 fusion.12
  124.2 0.9 dynamic-slice_bitcast_fusion
  125.1 1.4 collective-permute-start
  126.6 0.2 reshape.149
  126.8 0.1 collective-permute-start.1
  126.9 2.1 %collective-permute-start.2 = (f32[1,32,1280]{2,1,0:T(8,128)}, f32[1,32,1280]{2,1,0:T(8,128)S(1)}, u32[]{:S(2)}, u32[]{:S(2)}) collective-permute-start(f32[1,32,1280]{2,1,0:T(8,128)} %get-tuple-element.17), channel_id=1, source_target_pairs={{0,12},{4,8},{8,4},{12,0},{16,28},{20,24},{24,20},{28,16},{1,13},{... | collective-permute-start | bytes 491528 | tf_op jit(solution)/shard_map/ppermute | solution.py:121
  128.9 0.2 collective-permute-start.3
  129.2 3.5 %collective-permute-start.4 = (f32[1,32,1280]{2,1,0:T(8,128)S(1)}, f32[1,32,1280]{2,1,0:T(8,128)S(1)}, u32[]{:S(2)}, u32[]{:S(2)}) collective-permute-start(f32[1,32,1280]{2,1,0:T(8,128)S(1)} %get-tuple-element.15), channel_id=1, source_target_pairs={{0,20},{4,16},{8,28},{12,24},{16,4},{20,0},{24,12},{28,8},{1,21},{... | collective-permute-start | bytes 491528 | tf_op jit(solution)/shard_map/ppermute | solution.py:121
  132.7 1.5 collective-permute-start.5
  134.2 1.6 bitcast_dynamic-update-slice_fusion.16
  135.8 2.8 %collective-permute-done.1 = f32[1,32,1280]{2,1,0:T(8,128)S(1)} collective-permute-done((f32[1,32,1280]{2,1,0:T(8,128)}, f32[1,32,1280]{2,1,0:T(8,128)S(1)}, u32[]{:S(2)}, u32[]{:S(2)}) %collective-permute-start.1) | collective-permute-done | bytes 163872 | tf_op jit(solution)/shard_map/ppermute | solution.py:121
  138.6 1.2 collective-permute-start.6
  139.8 0.7 bitcast_dynamic-update-slice_fusion.15
  140.5 0.0 collective-permute-done.2
  140.5 0.7 bitcast_dynamic-update-slice_fusion.14
  141.2 9.9 %collective-permute-done.3 = f32[1,32,1280]{2,1,0:T(8,128)S(1)} collective-permute-done((f32[1,32,1280]{2,1,0:T(8,128)S(1)}, f32[1,32,1280]{2,1,0:T(8,128)S(1)}, u32[]{:S(2)}, u32[]{:S(2)}) %collective-permute-start.3) | collective-permute-done | bytes 163872 | tf_op jit(solution)/shard_map/ppermute | solution.py:121
  151.0 0.7 bitcast_dynamic-update-slice_fusion.13
  151.7 3.7 %collective-permute-done.4 = f32[1,32,1280]{2,1,0:T(8,128)S(1)} collective-permute-done((f32[1,32,1280]{2,1,0:T(8,128)S(1)}, f32[1,32,1280]{2,1,0:T(8,128)S(1)}, u32[]{:S(2)}, u32[]{:S(2)}) %collective-permute-start.4) | collective-permute-done | bytes 163872 | tf_op jit(solution)/shard_map/ppermute | solution.py:121
  155.4 0.7 bitcast_dynamic-update-slice_fusion.12
  156.0 0.7 bitcast_dynamic-update-slice_fusion.11
  156.7 0.7 bitcast_dynamic-update-slice_fusion.10
  157.4 1.9 %gather_fusion = f32[8,32,1280]{2,1,0:T(8,128)S(1)} fusion(f32[8,32,1280]{2,1,0:T(8,128)} %bitcast.139, s32[1024]{0:T(1024)S(1)} %pad_clamp_fusion), kind=kCustom, calls=%fused_computation | custom fusion | bytes 2621472 | tf_op jit(solution)/shard_map/gather | solution.py:122
  159.4 1.8 %copy.28 = f32[1,32,8,1280]{3,2,1,0:T(8,128)} copy(f32[1,32,8,1280]{3,1,2,0:T(8,128)S(1)} %bitcast.138) | data formatting | bytes 2621440 | tf_op jit(solution)/shard_map/transpose | solution.py:14
  161.2 1.5 reshape_reshape.3
  162.7 2.0 %fusion.1 = f32[5,1,32,2048]{3,2,1,0:T(8,128)} fusion(f32[5,1,32,2048]{3,2,1,0:T(8,128)S(1)} %reshape.149, f32[1,32,5,2048]{3,2,1,0:T(8,128)S(1)} %reshape_reshape.3), kind=kLoop, calls=%fused_computation.5 | loop fusion | flops 655360 | bytes 3932160 | tf_op jit(solution)/shard_map/neg | solution.py:125
  (26 shorter events, 0.5 us)
Async XLA Ops:
  0.0 2.5 %copy-start = (f32[3,1,32,2048]{3,2,1,0:T(8,128)S(1)}, f32[3,1,32,2048]{3,2,1,0:T(8,128)}, u32[]{:S(2)}) copy-start(f32[3,1,32,2048]{3,2,1,0:T(8,128)} %param.6) | copy-start | bytes 2359300
  1.0 1.5 copy-start.2
  1.1 1.5 copy-start.3
  59.6 38.7 %all-to-all-start = ((f32[8,1,40960]{2,1,0:T(1,128)}), f32[8,1,40960]{2,1,0:T(1,128)S(1)}, u32[]{:S(2)}, u32[]{:S(2)}) async-start(f32[8,1,40960]{2,1,0:T(1,128)} %reshape.167), calls=%async_computation | async-start | bytes 2621440 | tf_op jit(solution)/shard_map/all_to_all | solution.py:114
  67.3 0.9 copy-start.5
  122.0 1.0 copy-start.4
  124.2 2.3 %copy-start.1 = (f32[5,1,32,16,128]{4,3,2,0,1:T(8,128)S(1)}, f32[5,1,32,16,128]{4,3,2,0,1:T(8,128)}, u32[]{:S(2)}) copy-start(f32[5,1,32,16,128]{4,3,2,0,1:T(8,128)} %fusion) | copy-start | bytes 3932164
  125.1 7.6 %collective-permute-start = (f32[1,32,1280]{2,1,0:T(8,128)}, f32[1,32,1280]{2,1,0:T(8,128)}, u32[]{:S(2)}, u32[]{:S(2)}) collective-permute-start(f32[1,32,1280]{2,1,0:T(8,128)} %get-tuple-element.19), channel_id=1, source_target_pairs={{0,4},{4,0},{8,12},{12,8},{16,20},{20,16},{24,28},{28,24},{1,5},{5... | collective-permute-start | bytes 491528 | tf_op jit(solution)/shard_map/ppermute | solution.py:121
  126.8 11.8 %collective-permute-start.1 = (f32[1,32,1280]{2,1,0:T(8,128)}, f32[1,32,1280]{2,1,0:T(8,128)S(1)}, u32[]{:S(2)}, u32[]{:S(2)}) collective-permute-start(f32[1,32,1280]{2,1,0:T(8,128)} %get-tuple-element.18), channel_id=1, source_target_pairs={{0,8},{4,12},{8,0},{12,4},{16,24},{20,28},{24,16},{28,20},{1,9},{5... | collective-permute-start | bytes 491528 | tf_op jit(solution)/shard_map/ppermute | solution.py:121
  126.9 13.6 %collective-permute-start.2 = (f32[1,32,1280]{2,1,0:T(8,128)}, f32[1,32,1280]{2,1,0:T(8,128)S(1)}, u32[]{:S(2)}, u32[]{:S(2)}) collective-permute-start(f32[1,32,1280]{2,1,0:T(8,128)} %get-tuple-element.17), channel_id=1, source_target_pairs={{0,12},{4,8},{8,4},{12,0},{16,28},{20,24},{24,20},{28,16},{1,13},{... | collective-permute-start | bytes 491528 | tf_op jit(solution)/shard_map/ppermute | solution.py:121
  128.9 22.1 %collective-permute-start.3 = (f32[1,32,1280]{2,1,0:T(8,128)S(1)}, f32[1,32,1280]{2,1,0:T(8,128)S(1)}, u32[]{:S(2)}, u32[]{:S(2)}) collective-permute-start(f32[1,32,1280]{2,1,0:T(8,128)S(1)} %get-tuple-element.16), channel_id=1, source_target_pairs={{0,16},{4,20},{8,24},{12,28},{16,0},{20,4},{24,8},{28,12},{1,17},{... | collective-permute-start | bytes 491528 | tf_op jit(solution)/shard_map/ppermute | solution.py:121
  129.2 26.2 %collective-permute-start.4 = (f32[1,32,1280]{2,1,0:T(8,128)S(1)}, f32[1,32,1280]{2,1,0:T(8,128)S(1)}, u32[]{:S(2)}, u32[]{:S(2)}) collective-permute-start(f32[1,32,1280]{2,1,0:T(8,128)S(1)} %get-tuple-element.15), channel_id=1, source_target_pairs={{0,20},{4,16},{8,28},{12,24},{16,4},{20,0},{24,12},{28,8},{1,21},{... | collective-permute-start | bytes 491528 | tf_op jit(solution)/shard_map/ppermute | solution.py:121
  132.7 23.3 %collective-permute-start.5 = (f32[1,32,1280]{2,1,0:T(8,128)S(1)}, f32[1,32,1280]{2,1,0:T(8,128)S(1)}, u32[]{:S(2)}, u32[]{:S(2)}) collective-permute-start(f32[1,32,1280]{2,1,0:T(8,128)S(1)} %get-tuple-element.14), channel_id=1, source_target_pairs={{0,24},{4,28},{8,16},{12,20},{16,8},{20,12},{24,0},{28,4},{1,25},{... | collective-permute-start | bytes 491528 | tf_op jit(solution)/shard_map/ppermute | solution.py:121
  138.6 18.1 %collective-permute-start.6 = (f32[1,32,1280]{2,1,0:T(8,128)S(1)}, f32[1,32,1280]{2,1,0:T(8,128)S(1)}, u32[]{:S(2)}, u32[]{:S(2)}) collective-permute-start(f32[1,32,1280]{2,1,0:T(8,128)S(1)} %get-tuple-element.13), channel_id=1, source_target_pairs={{0,28},{4,24},{8,20},{12,16},{16,12},{20,8},{24,4},{28,0},{1,29},{... | collective-permute-start | bytes 491528 | tf_op jit(solution)/shard_map/ppermute | solution.py:121
